TPU v7x, 32 devices: a whole 2x2x4 slice. The times are simulated.
32 devices in a mesh: blk: 4 (over z), rows: 8 (over y, x, core).
Axes of the slice: x: 2, y: 2, z: 4, core: 2. Of those that a mesh axis runs over, the one named last changes fastest.
Arguments:
- features: bfloat16 [4, 4096, 2048], P(None, ('blk', 'rows')), may hold values from -6 to 6
- owner_ids: int32 [4096, 1], P(('blk', 'rows')), may hold values from 0 to 7; in each aligned block of 128 rows (0 to 127, 128 to 255, ...) at most 32 rows name the same one
- test_blocks: bfloat16 [4, 192, 2048], P(None, 'blk'), may hold values from -0.0625 to 0.0625
Outputs:
- scores: bfloat16 [8192, 192], P(('blk', 'rows'))
Inputs may be any that keep to these rules, and one draw needn't show every extreme that they name: `owner_ids`: within each aligned block of 128 rows (the rows of one device) no owner is named more than 32 times.
All inputs are finite; a program needn't handle non-finite values.
Results may differ from a plain program's by a relative error of at most 0.001.
Values may be sent and summed in bfloat16 or wider, within the bound.
No kernel may reach another device: no remote copies, remote signals or barrier semaphores. Data moves between devices by JAX's collectives and lax.ppermute only.
A program may use at most 128 MiB of HBM per device.

v0:
```python
import jax
import jax.numpy as jnp
from jax import lax
from jax.sharding import PartitionSpec as P


def slot_matrix(owner_ids, owners_n, capacity):
    owner = owner_ids[:, 0]
    onehot = (owner[:, None] == jnp.arange(owners_n, dtype=jnp.int32)[None, :]).astype(jnp.int32)
    before = jnp.cumsum(onehot, axis=0) - onehot
    rank = jnp.sum(before * onehot, axis=1)
    slot = owner * capacity + rank
    slots = jnp.arange(owners_n * capacity, dtype=jnp.int32)
    return (slots[:, None] == slot[None, :]).astype(jnp.bfloat16)


def on_device(features, owner_ids, test_blocks):
    owners_n = lax.axis_size("rows")
    local_rows = features.shape[1]
    capacity = 2 * local_rows // owners_n
    tests = lax.all_gather(test_blocks, "blk", axis=1, tiled=True)
    total = jnp.einsum("rsk,rtk->st", features, tests, preferred_element_type=jnp.float32)
    row_scores = total.astype(jnp.bfloat16)
    placed = jnp.dot(
        slot_matrix(owner_ids, owners_n, capacity), row_scores, preferred_element_type=jnp.float32
    ).astype(jnp.bfloat16)
    return lax.all_to_all(placed, "rows", split_axis=0, concat_axis=0, tiled=True)


def solution(mesh):
    return jax.shard_map(
        on_device,
        mesh=mesh,
        in_specs=(P(None, ("blk", "rows"), None), P(("blk", "rows"), None), P(None, "blk", None)),
        out_specs=P(("blk", "rows"), None),
        check_vma=False,
    )
```

profile of v0, /device:TPU:0, one launch (start us, length us, event | category | flops | bytes accessed | tf_op | source)
XLA Modules:
  0.0 95.1 jit_solution(11568899653987399284)
XLA Ops:
  6.5 0.0 copy-start
  6.5 0.0 all-gather.2.cloned.1.call-start
  6.5 0.7 all-gather.2.cloned.1.call-update
  7.3 0.7 fusion.2
  8.0 0.2 reduce_window_sum.11
  8.2 0.8 select_reduce_fusion
  9.0 0.7 multiply_add_fusion
  9.7 65.4 %all-gather.2.cloned.1.call-done = bf16[4,192,2048]{2,1,0:T(8,128)(2,1)} async-done(((bf16[4,48,2048]{2,1,0:T(8,128)(2,1)}), bf16[4,192,2048]{2,1,0:T(8,128)(2,1)}) %all-gather.2.cloned.1.call-update) | async-done | bytes 3145744 | tf_op jit(solution)/shard_map/all_gather | solution.py:21
  75.1 0.0 copy-done
  75.1 3.4 %convolution_convert_fusion = bf16[256,192]{0,1:T(8,128)(2,1)S(1)} fusion(bf16[4,128,2048]{2,1,0:T(8,128)(2,1)S(1)} %copy-done, bf16[4,192,2048]{2,1,0:T(8,128)(2,1)} %all-gather.2.cloned.1.call-done, s32[128]{0:T(128)S(1)} %multiply_add_fusion), kind=kOutput, calls=%fused_computation | convolution fusion | flops 415342592 | bytes 5341696 | tf_op jit(solution)/shard_map/dot_general | solution.py:24
  78.5 0.1 copy.4
  78.6 8.9 %all_to_all.12 = bf16[8,32,192]{2,1,0:T(8,128)(2,1)S(1)} all-to-all(bf16[8,32,192]{2,1,0:T(8,128)(2,1)S(1)} %bitcast.12), channel_id=1, replica_groups=mesh['blk'=4,'rows'=8] {'rows'}, dimensions={0} | all-to-all | bytes 196608 | tf_op jit(solution)/shard_map/all_to_all | solution.py:27
  87.5 0.7 copy.5
Async XLA Ops:
  6.5 68.6 %copy-start = (bf16[4,128,2048]{2,1,0:T(8,128)(2,1)S(1)}, bf16[4,128,2048]{2,1,0:T(8,128)(2,1)}, u32[]{:S(2)}) copy-start(bf16[4,128,2048]{2,1,0:T(8,128)(2,1)} %param.3) | copy-start | bytes 6291460
  6.5 68.6 %all-gather.2.cloned.1.call-start = ((), (), s32[]{:S(2)}) async-start(), calls=%async_computation.1 | async-start | bytes 3932160 | tf_op jit(solution)/shard_map/all_gather | solution.py:21
Sparse Core Ops, SparseCore 0:
  8.9 66.1 all-gather.1
where the time goes:
time: 95.3 us; the launch traced here: 95.1 us
  waiting for transfers between devices  66.2 us (69%)
  between operations  13.4 us (14%)
  blocking collectives  8.93 us (9%)
  matrix products  3.37 us (4%)
  other arithmetic  2.4 us (3%)
    all_gather x1, waiting for transfers between devices, on_device(): tests = lax.all_gather(test_blocks, 'blk', axis=1, tiled=True)  65.4 us
    all_to_all x1, blocking collectives, on_device(): lax.all_to_all(placed, 'rows', split_axis=0, concat_axis=0, tiled=True)  8.93 us
    dot_general x1, matrix products, on_device(): jnp.dot(slot_matrix(owner_ids, owners_n, capacity), row_scores, preferred...  3.37 us
  transfers between devices with their start and end apart: 1, of which 1 were waited for; matrix products, arithmetic and copies ran while one was open for 3% of the time, Pallas kernels for 0%

commit v1 on v0

--- a/solution.py
+++ b/solution.py
@@ -18,7 +18,13 @@
     owners_n = lax.axis_size("rows")
     local_rows = features.shape[1]
     capacity = 2 * local_rows // owners_n
-    tests = lax.all_gather(test_blocks, "blk", axis=1, tiled=True)
+    size = lax.axis_size("blk")
+    held, blocks = (test_blocks, [test_blocks])
+    for _ in range(size - 1):
+        held = lax.ppermute(held, "blk", [(i, (i + 1) % size) for i in range(size)])
+        blocks.insert(0, held)
+    flat = jnp.concatenate(blocks, axis=1)
+    tests = jnp.roll(flat, (lax.axis_index("blk") + 1) * test_blocks.shape[1], axis=1)
     total = jnp.einsum("rsk,rtk->st", features, tests, preferred_element_type=jnp.float32)
     row_scores = total.astype(jnp.bfloat16)
     placed = jnp.dot(

time: 95.3 us -> 91.9 us (0.964)
  local copies, waits for them, and re-layouts: 0.85 us -> 16.3 us
  between operations: 13.4 us -> 0.05 us
  waiting for transfers between devices: 66.2 us -> 57.9 us
  starting transfers between devices: 0.01 us -> 3.03 us
    all_gather x1 -> x0, waiting for transfers between devices: 65.4 us -> none  [on_device(): tests = lax.all_gather(test_blocks, 'blk', axis=1, tiled=True)]
    ppermute x0 -> x3, waiting for transfers between devices: none -> 57.9 us  [on_device(): held = lax.ppermute(held, 'blk', [(i, (i + 1) % size) for i in range(size)])]
    unnamed x2 -> x15, local copies, waits for them, and re-layouts: 0.01 us -> 14.5 us
    ppermute x0 -> x3, starting transfers between devices: none -> 3.03 us  [on_device(): held = lax.ppermute(held, 'blk', [(i, (i + 1) % size) for i in range(size)])]
    concatenate x0 -> x1, local copies, waits for them, and re-layouts: none -> 0.99 us  [on_device(): jnp.roll(flat, (lax.axis_index('blk') + 1) * test_blocks.shape[1], axis=1)]
  transfers between devices with their start and end apart: 1 -> 3, of which waited for: 1 -> 3; matrix products, arithmetic and copies ran while one was open for 3% -> 3% of each run, Pallas kernels for 0% -> 0%
where the time goes in v1:
time: 91.9 us; the launch traced here: 91.4 us
  waiting for transfers between devices  57.9 us (63%)
  local copies, waits for them, and re-layouts  16.3 us (18%)
  blocking collectives  8.63 us (9%)
  matrix products  3.06 us (3%)
  starting transfers between devices  3.03 us (3%)
  other arithmetic  2.47 us (3%)
    ppermute x3, waiting for transfers between devices, on_device(): held = lax.ppermute(held, 'blk', [(i, (i + 1) % size) for i in range(size)])  57.9 us
    unnamed x15, local copies, waits for them, and re-layouts  14.5 us
    all_to_all x1, blocking collectives, on_device(): lax.all_to_all(placed, 'rows', split_axis=0, concat_axis=0, tiled=True)  8.63 us
    dot_general x1, matrix products, on_device(): jnp.dot(slot_matrix(owner_ids, owners_n, capacity), row_scores, preferred...  3.06 us
    ppermute x3, starting transfers between devices, on_device(): held = lax.ppermute(held, 'blk', [(i, (i + 1) % size) for i in range(size)])  3.03 us
  transfers between devices with their start and end apart: 3, of which 3 were waited for; matrix products, arithmetic and copies ran while one was open for 3% of the time, Pallas kernels for 0%

profile of v1, /device:TPU:0, one launch (start us, length us, event | category | flops | bytes accessed | tf_op | source)
XLA Modules:
  0.0 91.4 jit_solution(14133542217606283761)
XLA Ops:
  0.0 0.0 copy-start
  0.0 0.0 copy-start.1
  0.0 3.0 %collective-permute-start = (bf16[4,48,2048]{2,1,0:T(8,128)(2,1)}, bf16[4,48,2048]{2,1,0:T(8,128)(2,1)S(1)}, u32[]{:S(2)}, u32[]{:S(2)}) collective-permute-start(bf16[4,48,2048]{2,1,0:T(8,128)(2,1)} %param.5), channel_id=1, source_target_pairs={{0,8},{8,16},{16,24},{24,0},{1,9},{9,17},{17,25},{25,1},{2,10},{10... | collective-permute-start | bytes 2359304 | tf_op jit(solution)/shard_map/ppermute | solution.py:24
  3.0 19.8 %collective-permute-done = bf16[4,48,2048]{2,1,0:T(8,128)(2,1)S(1)} collective-permute-done((bf16[4,48,2048]{2,1,0:T(8,128)(2,1)}, bf16[4,48,2048]{2,1,0:T(8,128)(2,1)S(1)}, u32[]{:S(2)}, u32[]{:S(2)}) %collective-permute-start) | collective-permute-done | bytes 786464 | tf_op jit(solution)/shard_map/ppermute | solution.py:24
  22.8 0.0 copy-start.2
  22.8 0.9 copy-done.2
  23.7 0.0 collective-permute-start.1
  23.7 20.6 %collective-permute-done.1 = bf16[4,48,2048]{2,1,0:T(8,128)(2,1)} collective-permute-done((bf16[4,48,2048]{2,1,0:T(8,128)(2,1)S(1)}, bf16[4,48,2048]{2,1,0:T(8,128)(2,1)}, u32[]{:S(2)}, u32[]{:S(2)}) %collective-permute-start.1) | collective-permute-done | bytes 786464 | tf_op jit(solution)/shard_map/ppermute | solution.py:24
  44.3 0.0 collective-permute-start.2
  44.4 0.7 fusion.11
  45.1 0.2 reduce_window_sum.11
  45.3 0.0 copy-start.3
  45.3 0.9 select_reduce_fusion
  46.2 0.7 multiply_add_fusion
  46.8 17.4 %collective-permute-done.2 = bf16[4,48,2048]{2,1,0:T(8,128)(2,1)} collective-permute-done((bf16[4,48,2048]{2,1,0:T(8,128)(2,1)}, bf16[4,48,2048]{2,1,0:T(8,128)(2,1)}, u32[]{:S(2)}, u32[]{:S(2)}) %collective-permute-start.2) | collective-permute-done | bytes 786464 | tf_op jit(solution)/shard_map/ppermute | solution.py:24
  64.3 2.1 %constant_dynamic-update-slice_fusion.7 = bf16[4,384,2048]{2,1,0:T(8,128)(2,1)} fusion(bf16[4,48,2048]{2,1,0:T(8,128)(2,1)} %collective-permute-done.2), kind=kLoop, calls=%fused_computation.17 | loop fusion | bytes 1572864
  66.4 2.1 %constant_dynamic-update-slice_fusion.6 = bf16[4,384,2048]{2,1,0:T(8,128)(2,1)} fusion(bf16[4,384,2048]{2,1,0:T(8,128)(2,1)} %constant_dynamic-update-slice_fusion.7, bf16[4,48,2048]{2,1,0:T(8,128)(2,1)} %collective-permute-done.1), kind=kLoop, calls=%fused_computation.16 | loop fusion | bytes 1572864
  68.5 2.1 %constant_dynamic-update-slice_fusion.5 = bf16[4,384,2048]{2,1,0:T(8,128)(2,1)} fusion(bf16[4,384,2048]{2,1,0:T(8,128)(2,1)} %constant_dynamic-update-slice_fusion.6, bf16[4,48,2048]{2,1,0:T(8,128)(2,1)} %copy-done.2), kind=kLoop, calls=%fused_computation.15 | loop fusion | bytes 1572864
  70.6 2.1 %constant_dynamic-update-slice_fusion.4 = bf16[4,384,2048]{2,1,0:T(8,128)(2,1)} fusion(bf16[4,384,2048]{2,1,0:T(8,128)(2,1)} %constant_dynamic-update-slice_fusion.5, bf16[4,48,2048]{2,1,0:T(8,128)(2,1)} %param.5), kind=kLoop, calls=%fused_computation.14 | loop fusion | bytes 1572864
  72.7 2.1 %constant_dynamic-update-slice_fusion.3 = bf16[4,384,2048]{2,1,0:T(8,128)(2,1)} fusion(bf16[4,384,2048]{2,1,0:T(8,128)(2,1)} %constant_dynamic-update-slice_fusion.4, bf16[4,48,2048]{2,1,0:T(8,128)(2,1)} %collective-permute-done.2), kind=kLoop, calls=%fused_computation.13 | loop fusion | bytes 1572864
  74.8 2.1 %constant_dynamic-update-slice_fusion.2 = bf16[4,384,2048]{2,1,0:T(8,128)(2,1)} fusion(bf16[4,384,2048]{2,1,0:T(8,128)(2,1)} %constant_dynamic-update-slice_fusion.3, bf16[4,48,2048]{2,1,0:T(8,128)(2,1)} %collective-permute-done.1), kind=kLoop, calls=%fused_computation.12 | loop fusion | bytes 1572864
  76.9 0.0 copy-done.3
  76.9 0.9 %constant_dynamic-update-slice_fusion.1 = bf16[4,384,2048]{2,1,0:T(8,128)(2,1)} fusion(bf16[4,384,2048]{2,1,0:T(8,128)(2,1)} %constant_dynamic-update-slice_fusion.2, bf16[4,48,2048]{2,1,0:T(8,128)(2,1)S(1)} %copy-done.3), kind=kLoop, calls=%fused_computation.11 | loop fusion | bytes 1572864
  77.9 0.0 copy-done.1
  77.9 1.0 %constant_dynamic-update-slice_fusion = bf16[4,384,2048]{2,1,0:T(8,128)(2,1)} fusion(bf16[4,384,2048]{2,1,0:T(8,128)(2,1)} %constant_dynamic-update-slice_fusion.1, bf16[4,48,2048]{2,1,0:T(8,128)(2,1)S(1)} %copy-done.1), kind=kLoop, calls=%fused_computation.10 | loop fusion | bytes 1572864 | tf_op jit(solution)/shard_map/jit(_roll_dynamic)/concatenate | solution.py:27
  78.8 0.0 copy-done
  78.8 3.1 %convolution_convert_fusion = bf16[256,192]{0,1:T(8,128)(2,1)S(1)} fusion(bf16[4,128,2048]{2,1,0:T(8,128)(2,1)S(1)} %copy-done, bf16[4,384,2048]{2,1,0:T(8,128)(2,1)} %constant_dynamic-update-slice_fusion, s32[]{:T(128)S(6)} %select_n.14, s32[128]{0:T(128)S(1)} %multiply_add_fusion), kind=kOutput, calls=%fused_computation.2 | convolution fusion | flops 415342592 | bytes 5341700 | tf_op jit(solution)/shard_map/dot_general | solution.py:30
  81.9 0.1 copy.4
  82.0 8.6 %all_to_all.12 = bf16[8,32,192]{2,1,0:T(8,128)(2,1)S(1)} all-to-all(bf16[8,32,192]{2,1,0:T(8,128)(2,1)S(1)} %bitcast.11), channel_id=1, replica_groups=mesh['blk'=4,'rows'=8] {'rows'}, dimensions={0} | all-to-all | bytes 196608 | tf_op jit(solution)/shard_map/all_to_all | solution.py:33
  90.6 0.7 copy.5
Async XLA Ops:
  0.0 78.8 %copy-start = (bf16[4,128,2048]{2,1,0:T(8,128)(2,1)S(1)}, bf16[4,128,2048]{2,1,0:T(8,128)(2,1)}, u32[]{:S(2)}) copy-start(bf16[4,128,2048]{2,1,0:T(8,128)(2,1)} %param.3) | copy-start | bytes 6291460
  0.0 77.9 %copy-start.1 = (bf16[4,48,2048]{2,1,0:T(8,128)(2,1)S(1)}, bf16[4,48,2048]{2,1,0:T(8,128)(2,1)}, u32[]{:S(2)}) copy-start(bf16[4,48,2048]{2,1,0:T(8,128)(2,1)} %param.5) | copy-start | bytes 2359300
  0.0 22.8 %collective-permute-start = (bf16[4,48,2048]{2,1,0:T(8,128)(2,1)}, bf16[4,48,2048]{2,1,0:T(8,128)(2,1)S(1)}, u32[]{:S(2)}, u32[]{:S(2)}) collective-permute-start(bf16[4,48,2048]{2,1,0:T(8,128)(2,1)} %param.5), channel_id=1, source_target_pairs={{0,8},{8,16},{16,24},{24,0},{1,9},{9,17},{17,25},{25,1},{2,10},{10... | collective-permute-start | bytes 2359304 | tf_op jit(solution)/shard_map/ppermute | solution.py:24
  22.8 0.9 copy-start.2
  23.7 20.6 %collective-permute-start.1 = (bf16[4,48,2048]{2,1,0:T(8,128)(2,1)S(1)}, bf16[4,48,2048]{2,1,0:T(8,128)(2,1)}, u32[]{:S(2)}, u32[]{:S(2)}) collective-permute-start(bf16[4,48,2048]{2,1,0:T(8,128)(2,1)S(1)} %collective-permute-done), channel_id=1, source_target_pairs={{0,8},{8,16},{16,24},{24,0},{1,9},{9,17},{17,25},{25,1},{2,10},{10... | collective-permute-start | bytes 2359304 | tf_op jit(solution)/shard_map/ppermute | solution.py:24
  44.3 19.9 %collective-permute-start.2 = (bf16[4,48,2048]{2,1,0:T(8,128)(2,1)}, bf16[4,48,2048]{2,1,0:T(8,128)(2,1)}, u32[]{:S(2)}, u32[]{:S(2)}) collective-permute-start(bf16[4,48,2048]{2,1,0:T(8,128)(2,1)} %collective-permute-done.1), channel_id=1, source_target_pairs={{0,8},{8,16},{16,24},{24,0},{1,9},{9,17},{17,25},{25,1},{2,10},{10... | collective-permute-start | bytes 2359304 | tf_op jit(solution)/shard_map/ppermute | solution.py:24
  45.3 31.6 %copy-start.3 = (bf16[4,48,2048]{2,1,0:T(8,128)(2,1)S(1)}, bf16[4,48,2048]{2,1,0:T(8,128)(2,1)}, u32[]{:S(2)}) copy-start(bf16[4,48,2048]{2,1,0:T(8,128)(2,1)} %copy-done.2) | copy-start | bytes 2359300
